TPU v7x, 512 devices: a whole 4x8x8 slice. The times are simulated.
512 devices in a mesh: ens: 4 (over z_hi), lon: 32 (over z_lo, y, core), lat: 4 (over x).
Axes of the slice: x: 4, y: 8, z: 8 (z_hi: 4, z_lo: 2; z = z_hi * 2 + z_lo), core: 2. Of those that a mesh axis runs over, the one named last changes fastest.
Arguments:
- ocean_state: bfloat16 [4, 200, 32, 4096], P('ens', None, 'lat', 'lon'), may hold values from -6 to 6
- ocean_mask: int32 [32, 4096], P('lat', 'lon'), may hold values from 0 to 1, as said below
- dw_weight: float32 [200, 49], replicated, may hold values from -0.875 to 0.875
- norm_gain: float32 [200], replicated, may hold values from 0.1 to 1.9
- expand_weight: bfloat16 [200, 800], replicated, may hold values from -0.4375 to 0.4375
- reduce_weight: bfloat16 [800, 200], replicated, may hold values from -0.21875 to 0.21875
- cotangent: bfloat16 [4, 200, 32, 4096], P('ens', None, 'lat', 'lon'), may hold values from -6 to 6
Outputs:
- next_state: bfloat16 [4, 200, 32, 4096], P('ens', None, 'lat', 'lon')
- grad_depthwise: float32 [200, 49], replicated
- grad_gain: float32 [200], replicated
- grad_expand: float32 [200, 800], replicated
- grad_reduce: float32 [800, 200], replicated
Inputs may be any that keep to these rules, and one draw needn't show every extreme that they name: `ocean_mask`: the share of ocean cells differs from tile to tile of 8 x 128 cells, from about a third to nearly all.
All inputs are finite; a program needn't handle non-finite values.
Results may differ from a plain program's by a relative error of at most 0.0058.
Values may be sent and summed in bfloat16 or wider, within the bound.
No kernel may reach another device: no remote copies, remote signals or barrier semaphores. Data moves between devices by JAX's collectives and lax.ppermute only.
A program may use at most 64 MiB of HBM per device.

v0:
```python
import math
import jax
import jax.numpy as jnp
from jax import lax
from jax.sharding import PartitionSpec as P

KS = 7
norm_eps = 1e-06
root_half = 0.7071067811865476
gauss_norm = 0.3989422804014327


def with_halo(cells, sides, width):
    for axis, dim in sides:
        count = lax.axis_size(axis)
        head = lax.slice_in_dim(cells, 0, width, axis=dim)
        tail = lax.slice_in_dim(cells, cells.shape[dim] - width, cells.shape[dim], axis=dim)
        cells = jnp.concatenate(
            [
                lax.ppermute(tail, axis, [(i, (i + 1) % count) for i in range(count)]),
                cells,
                lax.ppermute(head, axis, [((i + 1) % count, i) for i in range(count)]),
            ],
            axis=dim,
        )
    return cells


def swapped(array, axis, stride):
    return lax.ppermute(array, axis, [(i, i ^ 1 << stride) for i in range(lax.axis_size(axis))])


def depthwise(padded, dw_weight, out_rows, out_cols):
    conv_sum = jnp.zeros((padded.shape[0], out_rows, out_cols), jnp.float32)
    for shift_a in range(KS):
        for shift_b in range(KS):
            tap_weight = dw_weight[:, shift_a * KS + shift_b][:, None, None]
            window = padded[:, shift_a : shift_a + out_rows, shift_b : shift_b + out_cols].astype(
                jnp.float32
            )
            conv_sum = conv_sum + tap_weight * window
    return conv_sum


def depthwise_grad(d_conv, padded, out_rows, out_cols):
    columns = []
    for shift_a in range(KS):
        for shift_b in range(KS):
            window = padded[:, shift_a : shift_a + out_rows, shift_b : shift_b + out_cols].astype(
                jnp.float32
            )
            columns.append(jnp.sum(d_conv * window, axis=(1, 2)))
    return jnp.stack(columns, axis=1)


def cell_pass(conv_blk, state_blk, cot_blk, mask_blk, norm_gain, expand_weight, reduce_weight):
    chan_mean = jnp.mean(conv_blk, axis=0, keepdims=True)
    centred = conv_blk - chan_mean
    chan_var = jnp.mean(centred * centred, axis=0, keepdims=True)
    inv_std = lax.rsqrt(chan_var + norm_eps)
    normed = centred * inv_std
    scaled = (normed * norm_gain[:, None]).astype(jnp.bfloat16)
    pre_act = jnp.dot(expand_weight.T, scaled, preferred_element_type=jnp.float32)
    normal_cdf = 0.5 * (1.0 + lax.erf(pre_act * root_half))
    normal_pdf = jnp.exp(-0.5 * pre_act * pre_act) * gauss_norm
    hidden = (pre_act * normal_cdf).astype(jnp.bfloat16)
    gelu_slope = normal_cdf + pre_act * normal_pdf
    branch = jnp.dot(reduce_weight.T, hidden, preferred_element_type=jnp.float32)
    out_blk = ((state_blk.astype(jnp.float32) + branch) * mask_blk[None, :]).astype(jnp.bfloat16)
    grad_reduce = jnp.dot(hidden, cot_blk.T, preferred_element_type=jnp.float32)
    d_hidden = jnp.dot(reduce_weight, cot_blk, preferred_element_type=jnp.float32)
    d_pre = (d_hidden * gelu_slope).astype(jnp.bfloat16)
    grad_expand = jnp.dot(scaled, d_pre.T, preferred_element_type=jnp.float32)
    d_scaled = jnp.dot(expand_weight, d_pre, preferred_element_type=jnp.float32)
    grad_gain = jnp.sum(d_scaled * normed, axis=1)
    d_normed = d_scaled * norm_gain[:, None]
    d_conv = inv_std * (
        d_normed
        - jnp.mean(d_normed, axis=0, keepdims=True)
        - normed * jnp.mean(d_normed * normed, axis=0, keepdims=True)
    )
    return (out_blk, d_conv, grad_expand, grad_reduce, grad_gain)


def body(ocean_state, ocean_mask, dw_weight, norm_gain, expand_weight, reduce_weight, cotangent):
    state_tile = ocean_state[0]
    channels = state_tile.shape[0]
    tile_rows = state_tile.shape[1]
    tile_cols = state_tile.shape[2]
    margin = KS // 2
    mask_bf = ocean_mask.astype(jnp.bfloat16)
    masked = state_tile * mask_bf[None]
    padded = with_halo(masked, (("lon", 2), ("lat", 1)), margin)
    lat_now = lax.axis_index("lat")
    lat_count = lax.axis_size("lat")
    lon_count = lax.axis_size("lon")
    top_strip = padded[:, tile_rows : tile_rows + margin, :][:, ::-1, ::-1]
    mirrored = top_strip
    for bit_number in range(lon_count.bit_length() - 1):
        mirrored = swapped(mirrored, "lon", bit_number)
    north_rows = jnp.where(lat_now == lat_count - 1, mirrored, padded[:, tile_rows + margin :, :])
    south_rows = jnp.where(lat_now == 0, jnp.zeros_like(top_strip), padded[:, :margin, :])
    padded = jnp.concatenate(
        [south_rows, padded[:, margin : tile_rows + margin, :], north_rows], axis=1
    )
    conv_out = depthwise(padded, dw_weight, tile_rows, tile_cols)
    cell_count = tile_rows * tile_cols
    cot_masked = (cotangent[0] * mask_bf[None]).reshape(channels, cell_count)
    out_flat, d_conv, grad_expand, grad_reduce, grad_gain = cell_pass(
        conv_out.reshape(channels, cell_count),
        state_tile.reshape(channels, cell_count),
        cot_masked,
        ocean_mask.astype(jnp.float32).reshape(cell_count),
        norm_gain,
        expand_weight,
        reduce_weight,
    )
    grad_depthwise = depthwise_grad(
        d_conv.reshape(channels, tile_rows, tile_cols), padded, tile_rows, tile_cols
    )
    grad_scale = 1.0 / math.sqrt(lax.axis_size("ens") * lat_count * lon_count * cell_count)
    grad_expand = grad_expand * grad_scale
    grad_reduce = grad_reduce * grad_scale
    grad_gain = grad_gain * grad_scale
    grad_depthwise = grad_depthwise * grad_scale
    grad_expand, grad_reduce, grad_gain, grad_depthwise = lax.psum(
        (grad_expand, grad_reduce, grad_gain, grad_depthwise), ("ens", "lon", "lat")
    )
    next_state = out_flat.reshape(channels, tile_rows, tile_cols)[None]
    return (next_state, grad_depthwise, grad_gain, grad_expand, grad_reduce)


def solution(mesh):
    return jax.shard_map(
        body,
        mesh=mesh,
        in_specs=(
            P("ens", None, "lat", "lon"),
            P("lat", "lon"),
            P(),
            P(),
            P(),
            P(),
            P("ens", None, "lat", "lon"),
        ),
        out_specs=(P("ens", None, "lat", "lon"), P(), P(), P(), P()),
        check_vma=False,
    )
```

profile of v0, /device:TPU:17, one launch (start us, length us, event | category | flops | bytes accessed | tf_op | source)
XLA Modules:
  0.0 393.7 jit_solution(8443036720947394535)
XLA Ops:
  7.2 0.0 copy-start
  7.2 0.0 all-reduce.4.cloned.1.call-start
  7.2 1.4 convert_bitcast_fusion
  8.6 1.3 copy.12
  9.9 0.2 bitcast_multiply_fusion.2
  10.1 3.8 collective-permute-start
  13.9 1.9 collective-permute-start.1
  15.8 3.1 collective-permute-done.1
  18.9 0.1 pad_maximum_fusion.3
  19.0 1.0 rev.3
  20.1 1.9 collective-permute-start.3
  22.0 1.4 collective-permute-done.3
  23.4 5.6 %collective-permute-start.4 = (bf16[200,3,134]{0,2,1:T(8,128)(2,1)S(1)}, bf16[200,3,134]{0,2,1:T(8,128)(2,1)S(1)}, u32[]{:S(2)}, u32[]{:S(2)}) collective-permute-start(bf16[200,3,134]{0,2,1:T(8,128)(2,1)S(1)} %collective-permute-done.3), channel_id=1, source_target_pairs={{0,8},{4,12},{8,0},{12,4},{16,24},{20,28},{24,16},{28,20},{32,40},... | collective-permute-start | bytes 482408 | tf_op jit(solution)/shard_map/ppermute | solution.py:30
  29.1 5.4 %collective-permute-done.4 = bf16[200,3,134]{0,2,1:T(8,128)(2,1)S(1)} collective-permute-done((bf16[200,3,134]{0,2,1:T(8,128)(2,1)S(1)}, bf16[200,3,134]{0,2,1:T(8,128)(2,1)S(1)}, u32[]{:S(2)}, u32[]{:S(2)}) %collective-permute-start.4) | collective-permute-done | bytes 160832 | tf_op jit(solution)/shard_map/ppermute | solution.py:30
  34.4 5.2 %collective-permute-start.5 = (bf16[200,3,134]{0,2,1:T(8,128)(2,1)S(1)}, bf16[200,3,134]{0,2,1:T(8,128)(2,1)S(1)}, u32[]{:S(2)}, u32[]{:S(2)}) collective-permute-start(bf16[200,3,134]{0,2,1:T(8,128)(2,1)S(1)} %collective-permute-done.4), channel_id=1, source_target_pairs={{0,16},{4,20},{8,24},{12,28},{16,0},{20,4},{24,8},{28,12},{32,48},... | collective-permute-start | bytes 482408 | tf_op jit(solution)/shard_map/ppermute | solution.py:30
  39.6 1.9 collective-permute-start.2
  41.5 7.3 %collective-permute-done.5 = bf16[200,3,134]{0,2,1:T(8,128)(2,1)S(1)} collective-permute-done((bf16[200,3,134]{0,2,1:T(8,128)(2,1)S(1)}, bf16[200,3,134]{0,2,1:T(8,128)(2,1)S(1)}, u32[]{:S(2)}, u32[]{:S(2)}) %collective-permute-start.5) | collective-permute-done | bytes 160832 | tf_op jit(solution)/shard_map/ppermute | solution.py:30
  48.9 1.9 collective-permute-start.6
  50.8 2.7 collective-permute-start.8
  53.5 9.6 %collective-permute-done.6 = bf16[200,3,134]{0,2,1:T(8,128)(2,1)S(1)} collective-permute-done((bf16[200,3,134]{0,2,1:T(8,128)(2,1)S(1)}, bf16[200,3,134]{0,2,1:T(8,128)(2,1)S(1)}, u32[]{:S(2)}, u32[]{:S(2)}) %collective-permute-start.6) | collective-permute-done | bytes 160832 | tf_op jit(solution)/shard_map/ppermute | solution.py:30
  63.1 1.9 collective-permute-start.7
  65.1 5.1 %collective-permute-done.7 = bf16[200,3,134]{0,2,1:T(8,128)(2,1)S(1)} collective-permute-done((bf16[200,3,134]{0,2,1:T(8,128)(2,1)S(1)}, bf16[200,3,134]{0,2,1:T(8,128)(2,1)S(1)}, u32[]{:S(2)}, u32[]{:S(2)}) %collective-permute-start.7) | collective-permute-done | bytes 160832 | tf_op jit(solution)/shard_map/ppermute | solution.py:30
  70.3 0.2 maximum_maximum_fusion
  70.5 8.3 %fusion.118 = (f32[8,128]{1,0:T(8,128)S(1)}, f32[200,8,128]{0,2,1:T(8,128)S(1)}) fusion(bf16[200,11,134]{0,2,1:T(8,128)(2,1)S(1)} %get-tuple-element.77, f32[200]{0:T(256)S(1)} %bitcast.303, f32[200]{0:T(256)S(1)} %bitcast.304, f32[200]{0:T(256)S(1)} %bitcast.257, f32[200]{0:T(256)S(1)} %bitcast.258, f32[200]{0:T(256)S(1)} %bitcast.259, ...), kind=kLoop, calls=%fused_computation.252 | loop fusion | flops 33790976 | bytes 18494496 | tf_op jit(solution)/shard_map/reduce_sum | solution.py:57
  78.8 0.4 multiply_reduce_fusion
  79.2 0.6 copy-done.1
  79.8 1.5 copy.62
  81.3 0.0 copy-start.47
  81.4 2.2 fusion.9
  83.6 1.7 fusion.5
  85.3 1.7 convolution_multiply_fusion.1
  87.0 1.3 multiply_reduce_fusion.1
  88.3 1.3 multiply_reduce_fusion.2
  89.6 1.5 copy.63
  91.1 3.8 fusion.59
  94.9 3.8 fusion.109
  98.6 1.6 convolution_multiply_fusion
  100.3 0.0 all-reduce.4.cloned.1.call-update
  100.3 0.0 copy-start.33
  100.3 3.0 fusion.91
  103.7 0.0 copy-start.46
  103.7 1.6 fusion.13
  105.3 0.8 copy.65
  106.5 0.2 stack.199
  106.7 106.2 %all-reduce = (f32[200,49]{0,1:T(8,128)}, f32[200]{0:T(256)}) all-reduce(f32[200,49]{0,1:T(8,128)S(1)} %broadcast_multiply_fusion, f32[200]{0:T(256)S(1)} %broadcast_multiply_fusion.4), channel_id=1, replica_groups=mesh['ens'=4,'lon'=32,'lat'=4] {'ens','lon','lat'}, use_global_device_ids=true, to_apply=%region_53.54 | all-reduce | flops 10000 | bytes 80000 | tf_op jit(solution)/shard_map/psum | solution.py:126
  212.9 171.0 %all-reduce.4.cloned.1.call-done = (f32[200,800]{1,0:T(8,128)}, f32[800,200]{0,1:T(8,128)}) async-done(((f32[200,800]{1,0:T(8,128)}, f32[800,200]{0,1:T(8,128)}), (f32[200,800]{1,0:T(8,128)}, f32[800,200]{0,1:T(8,128)})) %all-reduce.4.cloned.1.call-update) | async-done | bytes 1280016 | tf_op jit(solution)/shard_map/psum | solution.py:126
  383.9 2.1 copy.74
  386.0 0.9 copy.75
  (109 shorter events, 0.4 us)
Async XLA Ops:
  7.2 74.2 %copy-start = (bf16[200,800]{1,0:T(8,128)(2,1)S(1)}, bf16[200,800]{1,0:T(8,128)(2,1)}, u32[]{:S(2)}) copy-start(bf16[200,800]{1,0:T(8,128)(2,1)} %param.11) | copy-start | bytes 960004
  7.2 376.7 %all-reduce.4.cloned.1.call-start = ((), (), s32[]{:S(2)}) async-start(), calls=%async_computation | async-start | bytes 2867200 | tf_op jit(solution)/shard_map/psum | solution.py:126
  8.6 20.4 %copy-start.7 = (f32[200,49]{0,1:T(8,128)S(1)}, f32[200,49]{0,1:T(8,128)}, u32[]{:S(2)}) copy-start(f32[200,49]{0,1:T(8,128)} %param.9) | copy-start | bytes 117604
  10.1 5.7 %collective-permute-start = (bf16[200,8,3]{0,2,1:T(4,128)(2,1)S(1)}, bf16[200,8,3]{0,2,1:T(4,128)(2,1)S(1)}, u32[]{:S(2)}, u32[]{:S(2)}) collective-permute-start(bf16[200,8,3]{0,2,1:T(4,128)(2,1)S(1)} %get-tuple-element.80), channel_id=1, source_target_pairs={{0,4},{4,8},{8,12},{12,16},{16,20},{20,24},{24,28},{28,32},{32,36}... | collective-permute-start | bytes 28808 | tf_op jit(solution)/shard_map/ppermute | solution.py:20
  13.9 5.1 %collective-permute-start.1 = (bf16[200,8,3]{0,2,1:T(4,128)(2,1)S(1)}, bf16[200,8,3]{0,2,1:T(4,128)(2,1)S(1)}, u32[]{:S(2)}, u32[]{:S(2)}) collective-permute-start(bf16[200,8,3]{0,2,1:T(4,128)(2,1)S(1)} %get-tuple-element.81), channel_id=1, source_target_pairs={{4,0},{8,4},{12,8},{16,12},{20,16},{24,20},{28,24},{32,28},{36,32}... | collective-permute-start | bytes 28808 | tf_op jit(solution)/shard_map/ppermute | solution.py:22
  20.1 3.4 collective-permute-start.3
  23.4 11.0 %collective-permute-start.4 = (bf16[200,3,134]{0,2,1:T(8,128)(2,1)S(1)}, bf16[200,3,134]{0,2,1:T(8,128)(2,1)S(1)}, u32[]{:S(2)}, u32[]{:S(2)}) collective-permute-start(bf16[200,3,134]{0,2,1:T(8,128)(2,1)S(1)} %collective-permute-done.3), channel_id=1, source_target_pairs={{0,8},{4,12},{8,0},{12,4},{16,24},{20,28},{24,16},{28,20},{32,40},... | collective-permute-start | bytes 482408 | tf_op jit(solution)/shard_map/ppermute | solution.py:30
  34.4 14.5 %collective-permute-start.5 = (bf16[200,3,134]{0,2,1:T(8,128)(2,1)S(1)}, bf16[200,3,134]{0,2,1:T(8,128)(2,1)S(1)}, u32[]{:S(2)}, u32[]{:S(2)}) collective-permute-start(bf16[200,3,134]{0,2,1:T(8,128)(2,1)S(1)} %collective-permute-done.4), channel_id=1, source_target_pairs={{0,16},{4,20},{8,24},{12,28},{16,0},{20,4},{24,8},{28,12},{32,48},... | collective-permute-start | bytes 482408 | tf_op jit(solution)/shard_map/ppermute | solution.py:30
  39.6 25.5 %collective-permute-start.2 = (bf16[200,3,134]{0,2,1:T(8,128)(2,1)S(1)}, bf16[200,3,134]{0,2,1:T(8,128)(2,1)S(1)}, u32[]{:S(2)}, u32[]{:S(2)}) collective-permute-start(bf16[200,3,134]{0,2,1:T(8,128)(2,1)S(1)} %get-tuple-element.79), channel_id=1, source_target_pairs={{0,1},{1,2},{2,3},{3,0},{4,5},{5,6},{6,7},{7,4},{8,9},{9,10},{10,1... | collective-permute-start | bytes 482408 | tf_op jit(solution)/shard_map/ppermute | solution.py:20
  48.9 14.3 %collective-permute-start.6 = (bf16[200,3,134]{0,2,1:T(8,128)(2,1)S(1)}, bf16[200,3,134]{0,2,1:T(8,128)(2,1)S(1)}, u32[]{:S(2)}, u32[]{:S(2)}) collective-permute-start(bf16[200,3,134]{0,2,1:T(8,128)(2,1)S(1)} %collective-permute-done.5), channel_id=1, source_target_pairs={{0,32},{4,36},{8,40},{12,44},{16,48},{20,52},{24,56},{28,60},{32,0... | collective-permute-start | bytes 482408 | tf_op jit(solution)/shard_map/ppermute | solution.py:30
  50.8 14.3 %collective-permute-start.8 = (bf16[200,3,134]{0,2,1:T(8,128)(2,1)S(1)}, bf16[200,3,134]{0,2,1:T(8,128)(2,1)S(1)}, u32[]{:S(2)}, u32[]{:S(2)}) collective-permute-start(bf16[200,3,134]{0,2,1:T(8,128)(2,1)S(1)} %get-tuple-element.78), channel_id=1, source_target_pairs={{1,0},{2,1},{3,2},{0,3},{5,4},{6,5},{7,6},{4,7},{9,8},{10,9},{11,1... | collective-permute-start | bytes 482408 | tf_op jit(solution)/shard_map/ppermute | solution.py:22
  63.1 7.1 %collective-permute-start.7 = (bf16[200,3,134]{0,2,1:T(8,128)(2,1)S(1)}, bf16[200,3,134]{0,2,1:T(8,128)(2,1)S(1)}, u32[]{:S(2)}, u32[]{:S(2)}) collective-permute-start(bf16[200,3,134]{0,2,1:T(8,128)(2,1)S(1)} %collective-permute-done.6), channel_id=1, source_target_pairs={{0,64},{4,68},{8,72},{12,76},{16,80},{20,84},{24,88},{28,92},{32,9... | collective-permute-start | bytes 482408 | tf_op jit(solution)/shard_map/ppermute | solution.py:30
  94.8 3.8 copy-start.2
  94.8 3.8 copy-start.48
  100.3 3.1 copy-start.3
  100.3 3.1 copy-start.5
  100.3 3.1 copy-start.33
  103.4 2.8 copy-start.9
  103.4 2.8 copy-start.10
  103.4 2.8 copy-start.11
  103.4 2.8 copy-start.12
  103.4 2.8 copy-start.13
  103.4 2.8 copy-start.14
  103.4 2.8 copy-start.15
  103.4 2.8 copy-start.16
  103.5 2.8 copy-start.17
  103.5 2.8 copy-start.18
  103.5 2.8 copy-start.19
  103.5 2.8 copy-start.20
  103.5 2.8 copy-start.21
  103.5 2.8 copy-start.22
  103.5 2.8 copy-start.23
  103.5 2.8 copy-start.24
  103.5 2.8 copy-start.25
  103.5 2.8 copy-start.26
  103.6 2.8 copy-start.27
  103.6 2.8 copy-start.28
  103.6 2.8 copy-start.29
  103.6 2.8 copy-start.30
  103.6 2.8 copy-start.31
  103.6 2.8 copy-start.32
  103.6 2.8 copy-start.34
  103.6 2.8 copy-start.35
  103.6 2.8 copy-start.36
  103.6 2.8 copy-start.37
  103.7 2.8 copy-start.38
  103.7 2.8 copy-start.39
  103.7 2.9 copy-start.46
  (12 other events, 28.0 us)
Sparse Core Ops, SparseCore 0:
  100.4 283.4 all-reduce.3
where the time goes:
time: 394 us
  waiting for transfers between devices  203 us (52%)
  blocking collectives  106 us (27%)
  starting transfers between devices  26.9 us (7%)
  other arithmetic  22.5 us (6%)
  between operations  14.9 us (4%)
  matrix products  10.2 us (3%)
  local copies, waits for them, and re-layouts  10.1 us (3%)
    psum x1, waiting for transfers between devices, body(): lax.psum((grad_expand, grad_reduce, grad_gain, grad_depthwise), ('ens', '...  171 us
    psum x1, blocking collectives, body(): lax.psum((grad_expand, grad_reduce, grad_gain, grad_depthwise), ('ens', '...  106 us
    ppermute x5, waiting for transfers between devices, swapped(): lax.ppermute(array, axis, [(i, i ^ 1 << stride) for i in range(lax.axis_s...  28.8 us
    ppermute x5, starting transfers between devices, swapped(): lax.ppermute(array, axis, [(i, i ^ 1 << stride) for i in range(lax.axis_s...  16.5 us
    reduce_sum x4, other arithmetic, depthwise_grad(): columns.append(jnp.sum(d_conv * window, axis=(1, 2)))  11.9 us
    reduce_sum x1, other arithmetic, cell_pass(): chan_mean = jnp.mean(conv_blk, axis=0, keepdims=True)  8.28 us
  transfers between devices with their start and end apart: 10, of which 7 were waited for; matrix products, arithmetic and copies ran while one was open for 1% of the time, Pallas kernels for 0%

commit v1 on v0

--- a/solution.py
+++ b/solution.py
@@ -124,7 +124,7 @@
     grad_gain = grad_gain * grad_scale
     grad_depthwise = grad_depthwise * grad_scale
     grad_expand, grad_reduce, grad_gain, grad_depthwise = lax.psum(
-        (grad_expand, grad_reduce, grad_gain, grad_depthwise), ("ens", "lon", "lat")
+        lax.psum((grad_expand, grad_reduce, grad_gain, grad_depthwise), ("lon", "lat")), "ens"
     )
     next_state = out_flat.reshape(channels, tile_rows, tile_cols)[None]
     return (next_state, grad_depthwise, grad_gain, grad_expand, grad_reduce)

time: 394 us -> 1730 us (4.39)
  the two profiles are of different devices: /device:TPU:17 before, /device:TPU:64 now
where the time goes in v1:
time: 1730 us
  waiting for transfers between devices  1070 us (62%)
  blocking collectives  573 us (33%)
  starting transfers between devices  35.6 us (2%)
  other arithmetic  20 us (1%)
    psum x1, waiting for transfers between devices, body(): lax.psum((grad_expand, grad_reduce, grad_gain, grad_depthwise), ('lon', '...  1040 us
    psum x1, blocking collectives, body(): lax.psum((grad_expand, grad_reduce, grad_gain, grad_depthwise), ('lon', '...  551 us
  transfers between devices with their start and end apart: 11, of which 7 were waited for; matrix products, arithmetic and copies ran while one was open for 1% of the time, Pallas kernels for 0%

profile of v1, /device:TPU:64, one launch (start us, length us, event | category | flops | bytes accessed | tf_op | source)
XLA Modules:
  0.0 1729.2 jit_solution(9163269346409145588)
XLA Ops:
  7.2 0.0 all-reduce.7.cloned.1.call-start
  7.2 0.8 convert_bitcast_fusion
  8.0 1.3 copy.12
  9.3 0.2 bitcast_multiply_fusion.2
  9.5 1.9 collective-permute-start
  11.4 5.8 collective-permute-start.1
  17.2 1.4 collective-permute-done.1
  18.6 0.1 pad_maximum_fusion.3
  18.7 1.0 rev.3
  19.7 1.9 collective-permute-start.3
  21.7 1.4 collective-permute-done.3
  23.1 2.7 collective-permute-start.4
  25.8 6.4 collective-permute-done.4
  32.2 6.2 collective-permute-start.5
  38.4 3.4 collective-permute-start.2
  41.8 6.2 collective-permute-done.5
  47.9 7.4 collective-permute-start.6
  55.3 2.0 collective-permute-start.8
  57.3 5.7 collective-permute-done.6
  63.1 4.2 collective-permute-start.7
  67.3 4.2 collective-permute-done.7
  71.6 0.2 maximum_maximum_fusion
  71.8 8.3 fusion.118
  80.2 0.4 multiply_reduce_fusion
  80.5 0.6 copy-done.1
  81.1 1.5 copy.62
  82.7 0.9 fusion.9
  83.6 0.1 copy-done.8
  83.7 0.1 copy-done.9
  83.8 1.7 fusion.5
  85.5 1.7 convolution_multiply_fusion.1
  87.2 1.6 multiply_reduce_fusion.1
  88.8 1.6 convolution_multiply_fusion
  90.5 2.3 fusion.13
  92.8 0.8 copy.65
  93.6 1.3 multiply_reduce_fusion.2
  94.9 1.5 copy.63
  96.3 0.0 all-reduce.7.cloned.1.call-update
  96.4 0.2 all-reduce.9.cloned.1.call-start
  96.6 2.4 fusion.91
  99.0 3.2 fusion.59
  102.2 1041.2 %all-reduce.7.cloned.1.call-done = (f32[200,800]{1,0:T(8,128)}, f32[800,200]{0,1:T(8,128)}) async-done(((f32[200,800]{1,0:T(8,128)}, f32[800,200]{0,1:T(8,128)}), (f32[200,800]{1,0:T(8,128)}, f32[800,200]{0,1:T(8,128)})) %all-reduce.7.cloned.1.call-update) | async-done | bytes 1280016 | tf_op jit(solution)/shard_map/psum | solution.py:127
  1143.4 3.2 fusion.109
  1146.5 0.2 stack.199
  1146.7 551.0 %all-reduce = (f32[200,49]{0,1:T(8,128)S(1)}, f32[200]{0:T(256)S(1)}) all-reduce(f32[200,49]{0,1:T(8,128)S(1)} %broadcast_multiply_fusion, f32[200]{0:T(256)S(1)} %broadcast_multiply_fusion.4), channel_id=1, replica_groups=mesh['ens'=4,'lon'=32,'lat'=4] {'lon','lat'}, use_global_device_ids=true, to_apply=%region_53.54 | all-reduce | flops 10000 | bytes 80000 | tf_op jit(solution)/shard_map/psum | solution.py:127
  1697.7 21.7 %all-reduce.2 = (f32[200,49]{0,1:T(8,128)}, f32[200]{0:T(256)}) all-reduce(f32[200,49]{0,1:T(8,128)S(1)} %get-tuple-element.68, f32[200]{0:T(256)S(1)} %get-tuple-element.69), channel_id=1, replica_groups=mesh['ens'=4,'lon'=32,'lat'=4] {'ens'}, use_global_device_ids=true, to_apply=%region_54.55 | all-reduce | flops 10000 | bytes 80000 | tf_op jit(solution)/shard_map/psum | solution.py:126
  1719.4 2.1 copy.76
  1721.5 0.9 copy.77
  (33 shorter events, 0.2 us)
Async XLA Ops:
  7.2 75.5 %copy-start = (bf16[200,800]{1,0:T(8,128)(2,1)S(1)}, bf16[200,800]{1,0:T(8,128)(2,1)}, u32[]{:S(2)}) copy-start(bf16[200,800]{1,0:T(8,128)(2,1)} %param.11) | copy-start | bytes 960004
  7.2 1136.2 %all-reduce.7.cloned.1.call-start = ((), (), s32[]{:S(2)}) async-start(), calls=%async_computation | async-start | bytes 2867200 | tf_op jit(solution)/shard_map/psum | solution.py:127
  8.0 17.8 %copy-start.6 = (f32[200,49]{0,1:T(8,128)S(1)}, f32[200,49]{0,1:T(8,128)}, u32[]{:S(2)}) copy-start(f32[200,49]{0,1:T(8,128)} %param.9) | copy-start | bytes 117604
  9.5 7.7 collective-permute-start
  11.4 7.2 collective-permute-start.1
  19.7 3.4 collective-permute-start.3
  23.1 9.1 collective-permute-start.4
  32.2 15.8 collective-permute-start.5
  38.4 28.9 %collective-permute-start.2 = (bf16[200,3,134]{0,2,1:T(8,128)(2,1)S(1)}, bf16[200,3,134]{0,2,1:T(8,128)(2,1)S(1)}, u32[]{:S(2)}, u32[]{:S(2)}) collective-permute-start(bf16[200,3,134]{0,2,1:T(8,128)(2,1)S(1)} %get-tuple-element.83), channel_id=1, source_target_pairs={{0,1},{1,2},{2,3},{3,0},{4,5},{5,6},{6,7},{7,4},{8,9},{9,10},{10,1... | collective-permute-start | bytes 482408 | tf_op jit(solution)/shard_map/ppermute | solution.py:20
  47.9 15.1 collective-permute-start.6
  55.3 12.0 collective-permute-start.8
  63.1 8.5 collective-permute-start.7
  80.1 1.0 copy-start.1
  80.1 2.5 copy-start.7
  82.7 1.0 copy-start.8
  82.7 1.1 copy-start.9
  83.6 5.2 copy-start.2
  90.4 3.1 copy-start.3
  90.4 3.1 copy-start.4
  96.4 1623.1 %all-reduce.9.cloned.1.call-start = ((), (), s32[]{:S(2)}) async-start(), calls=%async_computation.1 | async-start | bytes 2867200 | tf_op jit(solution)/shard_map/psum | solution.py:126
  1719.4 2.1 copy-start.5
Sparse Core Ops, SparseCore 0:
  96.5 1046.8 all-reduce.6
  1146.7 79.6 all-reduce.8
